TPU v7x, 128 devices: a whole 4x4x4 slice. The times are simulated.
128 devices in a mesh: dom: 16 (over x, z_hi, core), cls: 8 (over z_lo, y).
Axes of the slice: x: 4, y: 4, z: 4 (z_hi: 2, z_lo: 2; z = z_hi * 2 + z_lo), core: 2. Of those that a mesh axis runs over, the one named last changes fastest.
Arguments:
- particles: bfloat16 [2048, 16384], P(('dom', 'cls')), may hold values from -6 to 6
- averages: float32 [256, 16384], P('cls'), may hold values from -4 to 4
- prior_mass: float32 [256], P('cls'), may hold values from 1 to 8
- group_ids: int32 [4, 2048, 1], P(None, ('dom', 'cls')), may hold values from 0 to 7; in each aligned block of 16 rows (0 to 15, 16 to 31, ..., all dimensions but the last counted through in order) at most 6 rows name the same one
- class_ids: int32 [4, 2048], P(None, ('dom', 'cls')), may hold values from 0 to 31
- rot_ids: int32 [4, 2048], P(None, ('dom', 'cls')), may hold values from 0 to 63
- weights: bfloat16 [4, 2048], P(None, ('dom', 'cls')), may hold values from 0.25 to 4
- owners: int32 [4], replicated, may hold values from 0 to 7
Outputs:
- scores: float32 [4, 2048, 2048], P(None, ('dom', 'cls'))
- final_averages: float32 [256, 16384], P('cls')
Inputs may be any that keep to these rules, and one draw needn't show every extreme that they name: `group_ids`: in every step, at most 6 of the 16 particles of one device name one class group; in every step some device's particles reach 6 for some group.
All inputs are finite; a program needn't handle non-finite values.
Results may differ from a plain program's by a relative error of at most 0.0027.
Values may be sent and summed in bfloat16 or wider, within the bound.
No kernel may reach another device: no remote copies, remote signals or barrier semaphores. Data moves between devices by JAX's collectives and lax.ppermute only.
A program may use at most 256 MiB of HBM per device.

v0:
```python
import math
import jax
import jax.numpy as jnp
from jax import lax
from jax.sharding import PartitionSpec as P

RADII = 128
ANGLES = 128
ROT = 64
STEPS = 4
ASTEP = 2


def from_root(block, axis, owner):
    block = jnp.where(lax.axis_index(axis) == owner, block, jnp.zeros_like(block))
    return lax.psum(block, axis)


def rotate_each(images, shifts, angles):
    angle_idx = jnp.arange(angles, dtype=jnp.int32)
    index = (angle_idx[None, :] - shifts[:, None]) % angles
    return jnp.take_along_axis(images, index[:, None, :], axis=2)


def per_device(particles, averages, prior_mass, group_ids, class_ids, rot_ids, weights, owners):
    per_dev = particles.shape[0]
    pixels = particles.shape[1]
    groups = lax.axis_size("cls")
    per_group = averages.shape[0]
    capacity = per_dev * 3 // 8
    slots = groups * capacity
    cube = particles.reshape(per_dev, RADII, ANGLES)
    doubled = jnp.concatenate([cube, cube], axis=2)
    scale = 1.0 / math.sqrt(pixels)
    turns_block = min(ROT, max(8, 512 // per_dev))
    block_starts = list(range(0, ROT, turns_block))
    current = averages
    all_scores = []
    for step in range(STEPS):
        shifts = rot_ids[step] * ASTEP
        rotated = rotate_each(cube, shifts, ANGLES).reshape(per_dev, pixels)
        target = group_ids[step, :, 0]
        onehot_group = (target[:, None] == jnp.arange(groups, dtype=jnp.int32)[None, :]).astype(
            jnp.int32
        )
        rank = jnp.sum((jnp.cumsum(onehot_group, axis=0) - 1) * onehot_group, axis=1)
        slot_of = target * capacity + rank
        placing = (slot_of[None, :] == jnp.arange(slots, dtype=jnp.int32)[:, None]).astype(
            jnp.bfloat16
        )
        send_images = jnp.dot(placing, rotated, preferred_element_type=jnp.float32).astype(
            jnp.bfloat16
        )
        class_hot = (
            class_ids[step][:, None] == jnp.arange(per_group, dtype=jnp.int32)[None, :]
        ).astype(jnp.bfloat16)
        weighted_hot = class_hot * weights[step][:, None]
        send_weights = jnp.dot(placing, weighted_hot, preferred_element_type=jnp.float32).astype(
            jnp.bfloat16
        )
        got_images, got_weights = (
            lax.all_to_all(send_images, "cls", split_axis=0, concat_axis=0, tiled=True),
            lax.all_to_all(send_weights, "cls", split_axis=0, concat_axis=0, tiled=True),
        )
        partial_value = lax.dot_general(
            got_weights, got_images, (((0,), (0,)), ((), ())), preferred_element_type=jnp.float32
        )
        counts = jnp.sum(got_weights.astype(jnp.float32), axis=0)
        totals, mass = lax.psum((partial_value, counts), "dom")
        current = (prior_mass[:, None] * current + totals) / (prior_mass + mass)[:, None]
        refs = from_root(current.astype(jnp.bfloat16), "cls", owners[step])
        pieces = []
        for first in block_starts:
            count = min(turns_block, ROT - first)
            views = [
                doubled[:, :, ANGLES - turn * ASTEP : 2 * ANGLES - turn * ASTEP]
                for turn in range(first, first + count)
            ]
            rolled = jnp.stack(views, axis=1).reshape(per_dev * count, pixels)
            product = lax.dot_general(
                rolled, refs, (((1,), (1,)), ((), ())), preferred_element_type=jnp.float32
            )
            pieces.append(product.reshape(per_dev, count * per_group))
        stacked = jnp.concatenate(pieces, axis=1)
        all_scores.append(stacked * scale)
    return (jnp.stack(all_scores, axis=0), current)


def solution(mesh):
    return jax.shard_map(
        per_device,
        mesh=mesh,
        in_specs=(
            P(("dom", "cls"), None),
            P("cls", None),
            P("cls"),
            P(None, ("dom", "cls"), None),
            P(None, ("dom", "cls")),
            P(None, ("dom", "cls")),
            P(None, ("dom", "cls")),
            P(),
        ),
        out_specs=(P(None, ("dom", "cls"), None), P("cls", None)),
        check_vma=False,
    )
```

profile of v0, /device:TPU:1, one launch (start us, length us, event | category | flops | bytes accessed | tf_op | source)
XLA Modules:
  0.0 682.3 jit_solution(3866032299633491612)
XLA Ops:
  12.0 6.4 all-to-all-start.6
  20.8 11.1 %gather_fusion.3 = bf16[2048,128]{1,0:T(8,128)(2,1)S(1)} fusion(bf16[16,128,128]{1,2,0:T(8,128)(2,1)S(1)} %copy.50, s32[2048]{0:T(1024)S(1)} %get-tuple-element.115), kind=kCustom, calls=%fused_computation.3.clone | custom fusion | bytes 1064960 | tf_op jit(solution)/shard_map/jit(take_along_axis)/gather | solution.py:22
  34.1 5.1 all-to-all-start.4
  40.2 4.1 all-to-all-done.4
  48.6 4.0 all-to-all-done.2
  61.0 4.4 all-to-all-start.7
  65.3 11.1 %gather_fusion.2 = bf16[2048,128]{1,0:T(8,128)(2,1)S(1)} fusion(bf16[16,128,128]{1,2,0:T(8,128)(2,1)S(1)} %copy.50, s32[2048]{0:T(1024)S(1)} %get-tuple-element.116), kind=kCustom, calls=%fused_computation.2.clone | custom fusion | bytes 1064960 | tf_op jit(solution)/shard_map/jit(take_along_axis)/gather | solution.py:22
  79.0 13.3 %all-to-all-done.7 = bf16[8,6,16384]{2,1,0:T(8,128)(2,1)} async-done(((bf16[8,6,16384]{2,1,0:T(8,128)(2,1)}), bf16[8,6,16384]{2,1,0:T(8,128)(2,1)}, u32[]{:S(2)}, u32[]{:S(2)}) %all-to-all-start.7) | async-done | bytes 1572896 | tf_op jit(solution)/shard_map/all_to_all | solution.py:62
  92.4 4.3 all-to-all-start.5
  96.8 11.1 %gather_fusion.1 = bf16[2048,128]{1,0:T(8,128)(2,1)S(1)} fusion(bf16[16,128,128]{1,2,0:T(8,128)(2,1)S(1)} %copy.50, s32[2048]{0:T(1024)S(1)} %get-tuple-element.117), kind=kCustom, calls=%fused_computation.1.clone | custom fusion | bytes 1064960 | tf_op jit(solution)/shard_map/jit(take_along_axis)/gather | solution.py:22
  110.6 13.2 %all-to-all-done.5 = bf16[8,6,16384]{2,1,0:T(8,128)(2,1)} async-done(((bf16[8,6,16384]{2,1,0:T(8,128)(2,1)}), bf16[8,6,16384]{2,1,0:T(8,128)(2,1)}, u32[]{:S(2)}, u32[]{:S(2)}) %all-to-all-start.5) | async-done | bytes 1572896 | tf_op jit(solution)/shard_map/all_to_all | solution.py:62
  123.8 4.4 all-to-all-start.3
  128.2 11.1 %gather_fusion = bf16[2048,128]{1,0:T(8,128)(2,1)S(1)} fusion(bf16[16,128,128]{1,2,0:T(8,128)(2,1)S(1)} %copy.50, s32[2048]{0:T(1024)S(1)} %get-tuple-element.118), kind=kCustom, calls=%fused_computation.clone | custom fusion | bytes 1064960 | tf_op jit(solution)/shard_map/jit(take_along_axis)/gather | solution.py:22
  141.9 13.3 %all-to-all-done.3 = bf16[8,6,16384]{2,1,0:T(8,128)(2,1)} async-done(((bf16[8,6,16384]{2,1,0:T(8,128)(2,1)}), bf16[8,6,16384]{2,1,0:T(8,128)(2,1)}, u32[]{:S(2)}, u32[]{:S(2)}) %all-to-all-start.3) | async-done | bytes 1572896 | tf_op jit(solution)/shard_map/all_to_all | solution.py:62
  155.2 4.4 all-to-all-start.1
  167.7 4.0 convolution_bitcast_fusion.2
  171.6 15.1 %all-to-all-done.1 = bf16[8,6,16384]{2,1,0:T(8,128)(2,1)} async-done(((bf16[8,6,16384]{2,1,0:T(8,128)(2,1)}), bf16[8,6,16384]{2,1,0:T(8,128)(2,1)}, u32[]{:S(2)}, u32[]{:S(2)}) %all-to-all-start.1) | async-done | bytes 1572896 | tf_op jit(solution)/shard_map/all_to_all | solution.py:62
  216.0 34.7 %all-reduce = (f32[32]{0:T(128)S(1)}, f32[32]{0:T(128)S(1)}, f32[32]{0:T(128)S(1)}, f32[32]{0:T(128)S(1)}) all-reduce(f32[32]{0:T(128)S(1)} %convert_reduce_fusion, f32[32]{0:T(128)S(1)} %convert_reduce_fusion.1, f32[32]{0:T(128)S(1)} %convert_reduce_fusion.2, f32[32]{0:T(128)S(1)} %convert_reduce_fusion.3), channel_id=1, replica_groups=mesh['dom'=16,'cls'=8] {'dom'}, use_global_device_ids=true, to_apply=%region_22.24 | all-reduce | flops 128 | bytes 1024 | tf_op jit(solution)/shard_map/psum | solution.py:69
  250.7 146.9 %all-reduce.6.cloned.1.call-done = (f32[32,16384]{1,0:T(8,128)}, f32[32,16384]{1,0:T(8,128)}, f32[32,16384]{1,0:T(8,128)}, f32[32,16384]{1,0:T(8,128)}) async-done(((f32[32,16384]{1,0:T(8,128)}, f32[32,16384]{1,0:T(8,128)}, f32[32,16384]{1,0:T(8,128)}, f32[32,16384]{1,0:T(8,128)}), (f32[32,16384]{1,0:T(8,128)}, f32[32,16384]{1,0:T(8,128)}, f32[32,16384]{1,0:T(8,128)}, ...) | async-done | bytes 8388624 | tf_op jit(solution)/shard_map/psum | solution.py:69
  397.5 4.2 convert_select_fusion.2
  401.8 4.9 convert_select_fusion
  428.6 14.3 %copy.48 = bf16[16,32,128,128]{3,2,1,0:T(8,128)(2,1)} copy(bf16[16,32,128,128]{3,2,0,1:T(8,128)(2,1)} %get-tuple-element.21) | data formatting | bytes 33554432 | tf_op jit(solution)/shard_map/stack | solution.py:79
  442.9 14.2 %copy.55 = bf16[16,32,128,128]{3,2,1,0:T(8,128)(2,1)} copy(bf16[16,32,128,128]{3,2,0,1:T(8,128)(2,1)} %get-tuple-element.22) | data formatting | bytes 33554432 | tf_op jit(solution)/shard_map/stack | solution.py:79
  457.1 53.9 %all-reduce.8.cloned.1.call-done = (bf16[32,16384]{1,0:T(8,128)(2,1)}, bf16[32,16384]{1,0:T(8,128)(2,1)}, bf16[32,16384]{1,0:T(8,128)(2,1)}, bf16[32,16384]{1,0:T(8,128)(2,1)}) async-done(((bf16[32,16384]{1,0:T(8,128)(2,1)}, bf16[32,16384]{1,0:T(8,128)(2,1)}, bf16[32,16384]{1,0:T(8,128)(2,1)}, bf16[32,16384]{1,0:T(8,128)(2,1)}), (bf16[32,16384]{1,0:T(8,128)(2,1)}, bf16[32,16384]{1,0:T(8,128)(2,1)}, ...) | async-done | bytes 4194320 | tf_op jit(solution)/shard_map/psum | solution.py:16
  511.1 23.1 %fusion.14 = f32[512,32]{1,0:T(8,128)S(1)} fusion(bf16[32,16384]{1,0:T(8,128)(2,1)} %get-tuple-element.14, bf16[64,8,128,128]{3,2,1,0:T(8,128)(2,1)} %bitcast.404), kind=kOutput, calls=%fused_computation.26 | convolution fusion | flops 536870912 | bytes 17891328 | tf_op jit(solution)/shard_map/dot_general | solution.py:80
  534.2 21.5 %fusion.6 = f32[512,32]{1,0:T(8,128)S(1)} fusion(bf16[32,16384]{1,0:T(8,128)(2,1)} %get-tuple-element.14, bf16[64,8,128,128]{3,2,1,0:T(8,128)(2,1)} %bitcast.410), kind=kOutput, calls=%fused_computation.18 | convolution fusion | flops 536870912 | bytes 17891328 | tf_op jit(solution)/shard_map/dot_general | solution.py:80
  555.8 17.4 %fusion.12 = f32[512,32]{1,0:T(8,128)S(1)} fusion(bf16[32,16384]{1,0:T(8,128)(2,1)S(1)} %copy-done.3, bf16[64,8,128,128]{3,2,1,0:T(8,128)(2,1)S(1)} %bitcast.407), kind=kOutput, calls=%fused_computation.24 | convolution fusion | flops 536870912 | bytes 17891328 | tf_op jit(solution)/shard_map/dot_general | solution.py:80
  573.2 21.0 %fusion.4 = f32[512,32]{1,0:T(8,128)S(1)} fusion(bf16[32,16384]{1,0:T(8,128)(2,1)} %get-tuple-element.13, bf16[64,8,128,128]{3,2,1,0:T(8,128)(2,1)} %bitcast.411), kind=kOutput, calls=%fused_computation.16 | convolution fusion | flops 536870912 | bytes 17891328 | tf_op jit(solution)/shard_map/dot_general | solution.py:80
  594.2 18.6 %fusion.10 = f32[512,32]{1,0:T(8,128)S(1)} fusion(bf16[32,16384]{1,0:T(8,128)(2,1)} %get-tuple-element.12, bf16[64,8,128,128]{3,2,1,0:T(8,128)(2,1)S(1)} %bitcast.408), kind=kOutput, calls=%fused_computation.22 | convolution fusion | flops 536870912 | bytes 17891328 | tf_op jit(solution)/shard_map/dot_general | solution.py:80
  612.8 21.0 %fusion.2 = f32[512,32]{1,0:T(8,128)S(1)} fusion(bf16[32,16384]{1,0:T(8,128)(2,1)} %get-tuple-element.12, bf16[64,8,128,128]{3,2,1,0:T(8,128)(2,1)} %bitcast.412), kind=kOutput, calls=%fused_computation.14 | convolution fusion | flops 536870912 | bytes 17891328 | tf_op jit(solution)/shard_map/dot_general | solution.py:80
  633.8 18.4 %fusion.8 = f32[512,32]{1,0:T(8,128)S(1)} fusion(bf16[32,16384]{1,0:T(8,128)(2,1)} %get-tuple-element.11, bf16[64,8,128,128]{3,2,1,0:T(8,128)(2,1)S(1)} %bitcast.409), kind=kOutput, calls=%fused_computation.20 | convolution fusion | flops 536870912 | bytes 17891328 | tf_op jit(solution)/shard_map/dot_general | solution.py:80
  652.2 20.8 %fusion = f32[512,32]{1,0:T(8,128)S(1)} fusion(bf16[32,16384]{1,0:T(8,128)(2,1)} %get-tuple-element.11, bf16[64,8,128,128]{3,2,1,0:T(8,128)(2,1)} %bitcast.413), kind=kOutput, calls=%fused_computation.12 | convolution fusion | flops 536870912 | bytes 17891328 | tf_op jit(solution)/shard_map/dot_general | solution.py:80
  (130 shorter events, 89.6 us)
Async XLA Ops:
  12.0 22.1 %all-to-all-start.6 = ((bf16[8,6,32]{2,1,0:T(8,128)(2,1)}), bf16[8,6,32]{2,1,0:T(8,128)(2,1)S(1)}, u32[]{:S(2)}, u32[]{:S(2)}) async-start(bf16[8,6,32]{2,1,0:T(8,128)(2,1)} %all_to_all.60), calls=%async_computation.6 | async-start | bytes 32768 | tf_op jit(solution)/shard_map/all_to_all | solution.py:63
  34.1 10.2 %all-to-all-start.4 = ((bf16[8,6,32]{2,1,0:T(8,128)(2,1)}), bf16[8,6,32]{2,1,0:T(8,128)(2,1)S(1)}, u32[]{:S(2)}, u32[]{:S(2)}) async-start(bf16[8,6,32]{2,1,0:T(8,128)(2,1)} %all_to_all.56), calls=%async_computation.4 | async-start | bytes 32768 | tf_op jit(solution)/shard_map/all_to_all | solution.py:63
  44.3 8.3 %all-to-all-start.2 = ((bf16[8,6,32]{2,1,0:T(8,128)(2,1)}), bf16[8,6,32]{2,1,0:T(8,128)(2,1)S(1)}, u32[]{:S(2)}, u32[]{:S(2)}) async-start(bf16[8,6,32]{2,1,0:T(8,128)(2,1)} %all_to_all.52), calls=%async_computation.2 | async-start | bytes 32768 | tf_op jit(solution)/shard_map/all_to_all | solution.py:63
  52.6 8.3 %all-to-all-start = ((bf16[8,6,32]{2,1,0:T(8,128)(2,1)}), bf16[8,6,32]{2,1,0:T(8,128)(2,1)S(1)}, u32[]{:S(2)}, u32[]{:S(2)}) async-start(bf16[8,6,32]{2,1,0:T(8,128)(2,1)} %all_to_all.48), calls=%async_computation | async-start | bytes 32768 | tf_op jit(solution)/shard_map/all_to_all | solution.py:63
  61.0 31.4 %all-to-all-start.7 = ((bf16[8,6,16384]{2,1,0:T(8,128)(2,1)}), bf16[8,6,16384]{2,1,0:T(8,128)(2,1)}, u32[]{:S(2)}, u32[]{:S(2)}) async-start(bf16[8,6,16384]{2,1,0:T(8,128)(2,1)} %all_to_all.62), calls=%async_computation.7 | async-start | bytes 4194304 | tf_op jit(solution)/shard_map/all_to_all | solution.py:62
  92.4 31.4 %all-to-all-start.5 = ((bf16[8,6,16384]{2,1,0:T(8,128)(2,1)}), bf16[8,6,16384]{2,1,0:T(8,128)(2,1)}, u32[]{:S(2)}, u32[]{:S(2)}) async-start(bf16[8,6,16384]{2,1,0:T(8,128)(2,1)} %all_to_all.58), calls=%async_computation.5 | async-start | bytes 4194304 | tf_op jit(solution)/shard_map/all_to_all | solution.py:62
  123.8 31.4 %all-to-all-start.3 = ((bf16[8,6,16384]{2,1,0:T(8,128)(2,1)}), bf16[8,6,16384]{2,1,0:T(8,128)(2,1)}, u32[]{:S(2)}, u32[]{:S(2)}) async-start(bf16[8,6,16384]{2,1,0:T(8,128)(2,1)} %all_to_all.54), calls=%async_computation.3 | async-start | bytes 4194304 | tf_op jit(solution)/shard_map/all_to_all | solution.py:62
  155.2 31.5 %all-to-all-start.1 = ((bf16[8,6,16384]{2,1,0:T(8,128)(2,1)}), bf16[8,6,16384]{2,1,0:T(8,128)(2,1)}, u32[]{:S(2)}, u32[]{:S(2)}) async-start(bf16[8,6,16384]{2,1,0:T(8,128)(2,1)} %all_to_all.50), calls=%async_computation.1 | async-start | bytes 4194304 | tf_op jit(solution)/shard_map/all_to_all | solution.py:62
  159.6 31.0 %copy-start.1 = (s32[4]{0:T(128)S(1)}, s32[4]{0:T(128)}, u32[]{:S(2)}) copy-start(s32[4]{0:T(128)} %param.17) | copy-start | bytes 52
  159.6 237.9 %all-reduce.6.cloned.1.call-start = ((), (), s32[]{:S(2)}) async-start(), calls=%async_computation.8 | async-start | bytes 16777216 | tf_op jit(solution)/shard_map/psum | solution.py:69
  190.6 320.5 %all-reduce.8.cloned.1.call-start = ((), (), s32[]{:S(2)}) async-start(), calls=%async_computation.9 | async-start | bytes 8388608 | tf_op jit(solution)/shard_map/psum | solution.py:16
  194.0 56.7 %copy-start.2 = (f32[32]{0:T(128)S(1)}, f32[32]{0:T(128)}, u32[]{:S(2)}) copy-start(f32[32]{0:T(128)} %param.12) | copy-start | bytes 388
  195.2 202.3 %copy-start = (f32[32,16384]{1,0:T(8,128)S(1)}, f32[32,16384]{1,0:T(8,128)}, u32[]{:S(2)}) copy-start(f32[32,16384]{1,0:T(8,128)} %param.11) | copy-start | bytes 6291460
  511.1 44.7 %slice-start = ((s8[16777216]{0:T(1024)(128)(4,1)}), s8[4194304]{0:T(1024)(128)(4,1)S(1)}, s32[]{:S(2)}) async-start(s8[16777216]{0:T(1024)(128)(4,1)} %bitcast.405), calls=%async_computation.10 | async-start | bytes 8388608
  511.1 44.7 %slice-start.1 = ((s8[16777216]{0:T(1024)(128)(4,1)}), s8[4194304]{0:T(1024)(128)(4,1)S(1)}, s32[]{:S(2)}) async-start(s8[16777216]{0:T(1024)(128)(4,1)} %bitcast.405), calls=%async_computation.11 | async-start | bytes 8388608
  534.2 21.6 %copy-start.3 = (bf16[32,16384]{1,0:T(8,128)(2,1)S(1)}, bf16[32,16384]{1,0:T(8,128)(2,1)}, u32[]{:S(2)}) copy-start(bf16[32,16384]{1,0:T(8,128)(2,1)} %get-tuple-element.13) | copy-start | bytes 3145732
  534.2 21.6 %slice-start.2 = ((s8[16777216]{0:T(1024)(128)(4,1)}), s8[4194304]{0:T(1024)(128)(4,1)S(1)}, s32[]{:S(2)}) async-start(s8[16777216]{0:T(1024)(128)(4,1)} %bitcast.405), calls=%async_computation.12 | async-start | bytes 8388608
  534.2 21.6 %slice-start.3 = ((s8[16777216]{0:T(1024)(128)(4,1)}), s8[4194304]{0:T(1024)(128)(4,1)S(1)}, s32[]{:S(2)}) async-start(s8[16777216]{0:T(1024)(128)(4,1)} %bitcast.405), calls=%async_computation.13 | async-start | bytes 8388608
Sparse Core Ops, SparseCore 0:
  190.7 206.8 all-reduce.5
  406.8 104.1 all-reduce.7
where the time goes:
time: 691 us; the launch traced here: 682 us
  waiting for transfers between devices  266 us (38%)
  matrix products  182 us (26%)
  local copies, waits for them, and re-layouts  133 us (19%)
  starting transfers between devices  35.9 us (5%)
  blocking collectives  34.7 us (5%)
  between operations  17.4 us (3%)
  other arithmetic  13.8 us (2%)
    dot_general x8, matrix products, per_device(): lax.dot_general(rolled, refs, (((1,), (1,)), ((), ())), preferred_element...  162 us
    psum x1, waiting for transfers between devices, per_device(): totals, mass = lax.psum((partial_value, counts), 'dom')  147 us
    all_to_all x4, waiting for transfers between devices, per_device(): lax.all_to_all(send_images, 'cls', split_axis=0, concat_axis=0, tiled=True)  54.9 us
    psum x1, waiting for transfers between devices, from_root(): return lax.psum(block, axis)  53.9 us
    gather x8, local copies, waits for them, and re-layouts, rotate_each(): return jnp.take_along_axis(images, index[:, None, :], axis=2)  45.6 us
    unnamed x49, local copies, waits for them, and re-layouts  43.7 us
    psum x1, blocking collectives, per_device(): totals, mass = lax.psum((partial_value, counts), 'dom')  34.7 us
    another operation x3, local copies, waits for them, and re-layouts, per_device(): rolled = jnp.stack(views, axis=1).reshape(per_dev * count, pixels)  29.9 us
  transfers between devices with their start and end apart: 10, of which 9 were waited for; matrix products, arithmetic and copies ran while one was open for 20% of the time, Pallas kernels for 0%

commit v1 on v0

--- a/solution.py
+++ b/solution.py
@@ -13,7 +13,7 @@
 
 def from_root(block, axis, owner):
     block = jnp.where(lax.axis_index(axis) == owner, block, jnp.zeros_like(block))
-    return lax.psum(block, axis)
+    return jnp.sum(lax.all_gather(block, axis), axis=0)
 
 
 def rotate_each(images, shifts, angles):

time: 691 us -> 854 us (1.24)
  waiting for transfers between devices: 266 us -> 411 us
  other arithmetic: 13.8 us -> 33.7 us
  matrix products: 182 us -> 172 us
  local copies, waits for them, and re-layouts: 133 us -> 142 us
    all_gather x0 -> x4, waiting for transfers between devices: none -> 177 us  [from_root(): return jnp.sum(lax.all_gather(block, axis), axis=0)]
    psum x1 -> x0, waiting for transfers between devices: 53.9 us -> none  [from_root(): return lax.psum(block, axis)]
    reduce_sum x0 -> x4, other arithmetic: none -> 20.1 us  [from_root(): return jnp.sum(lax.all_gather(block, axis), axis=0)]
    psum x1, waiting for transfers between devices: 147 us -> 167 us  [per_device(): totals, mass = lax.psum((partial_value, counts), 'dom')]
    unnamed x49 -> x53, local copies, waits for them, and re-layouts: 43.7 us -> 43.7 us
  transfers between devices with their start and end apart: 10 -> 13, of which waited for: 9 -> 11; matrix products, arithmetic and copies ran while one was open for 20% -> 33% of each run, Pallas kernels for 0% -> 0%
where the time goes in v1:
time: 854 us; the launch traced here: 846 us
  waiting for transfers between devices  411 us (48%)
  matrix products  172 us (20%)
  local copies, waits for them, and re-layouts  142 us (17%)
  blocking collectives  35.9 us (4%)
  starting transfers between devices  35.3 us (4%)
  other arithmetic  33.7 us (4%)
  between operations  17.2 us (2%)
    all_gather x4, waiting for transfers between devices, from_root(): return jnp.sum(lax.all_gather(block, axis), axis=0)  177 us
    psum x1, waiting for transfers between devices, per_device(): totals, mass = lax.psum((partial_value, counts), 'dom')  167 us
    dot_general x8, matrix products, per_device(): lax.dot_general(rolled, refs, (((1,), (1,)), ((), ())), preferred_element...  154 us
    all_to_all x4, waiting for transfers between devices, per_device(): lax.all_to_all(send_images, 'cls', split_axis=0, concat_axis=0, tiled=True)  54.7 us
    gather x8, local copies, waits for them, and re-layouts, rotate_each(): return jnp.take_along_axis(images, index[:, None, :], axis=2)  45.6 us
    unnamed x53, local copies, waits for them, and re-layouts  43.7 us
    another operation x3, local copies, waits for them, and re-layouts, per_device(): rolled = jnp.stack(views, axis=1).reshape(per_dev * count, pixels)  38.2 us
    psum x1, blocking collectives, per_device(): totals, mass = lax.psum((partial_value, counts), 'dom')  35.9 us
  transfers between devices with their start and end apart: 13, of which 11 were waited for; matrix products, arithmetic and copies ran while one was open for 33% of the time, Pallas kernels for 0%

profile of v1, /device:TPU:1, one launch (start us, length us, event | category | flops | bytes accessed | tf_op | source)
XLA Modules:
  0.0 845.9 jit_solution(4089737253499171359)
XLA Ops:
  12.0 6.4 all-to-all-start.6
  20.8 11.1 %gather_fusion.3 = bf16[2048,128]{1,0:T(8,128)(2,1)S(1)} fusion(bf16[16,128,128]{1,2,0:T(8,128)(2,1)S(1)} %copy.50, s32[2048]{0:T(1024)S(1)} %get-tuple-element.111), kind=kCustom, calls=%fused_computation.3.clone | custom fusion | bytes 1064960 | tf_op jit(solution)/shard_map/jit(take_along_axis)/gather | solution.py:22
  33.3 5.1 all-to-all-start.4
  60.2 4.4 all-to-all-start.7
  64.6 11.1 %gather_fusion.2 = bf16[2048,128]{1,0:T(8,128)(2,1)S(1)} fusion(bf16[16,128,128]{1,2,0:T(8,128)(2,1)S(1)} %copy.50, s32[2048]{0:T(1024)S(1)} %get-tuple-element.112), kind=kCustom, calls=%fused_computation.2.clone | custom fusion | bytes 1064960 | tf_op jit(solution)/shard_map/jit(take_along_axis)/gather | solution.py:22
  78.3 13.3 %all-to-all-done.7 = bf16[8,6,16384]{2,1,0:T(8,128)(2,1)} async-done(((bf16[8,6,16384]{2,1,0:T(8,128)(2,1)}), bf16[8,6,16384]{2,1,0:T(8,128)(2,1)}, u32[]{:S(2)}, u32[]{:S(2)}) %all-to-all-start.7) | async-done | bytes 1572896 | tf_op jit(solution)/shard_map/all_to_all | solution.py:62
  96.1 11.1 %gather_fusion.1 = bf16[2048,128]{1,0:T(8,128)(2,1)S(1)} fusion(bf16[16,128,128]{1,2,0:T(8,128)(2,1)S(1)} %copy.50, s32[2048]{0:T(1024)S(1)} %get-tuple-element.113), kind=kCustom, calls=%fused_computation.1.clone | custom fusion | bytes 1064960 | tf_op jit(solution)/shard_map/jit(take_along_axis)/gather | solution.py:22
  109.8 13.2 %all-to-all-done.5 = bf16[8,6,16384]{2,1,0:T(8,128)(2,1)} async-done(((bf16[8,6,16384]{2,1,0:T(8,128)(2,1)}), bf16[8,6,16384]{2,1,0:T(8,128)(2,1)}, u32[]{:S(2)}, u32[]{:S(2)}) %all-to-all-start.5) | async-done | bytes 1572896 | tf_op jit(solution)/shard_map/all_to_all | solution.py:62
  123.0 4.4 all-to-all-start.3
  127.4 11.1 %gather_fusion = bf16[2048,128]{1,0:T(8,128)(2,1)S(1)} fusion(bf16[16,128,128]{1,2,0:T(8,128)(2,1)S(1)} %copy.50, s32[2048]{0:T(1024)S(1)} %get-tuple-element.114), kind=kCustom, calls=%fused_computation.clone | custom fusion | bytes 1064960 | tf_op jit(solution)/shard_map/jit(take_along_axis)/gather | solution.py:22
  141.2 13.3 %all-to-all-done.3 = bf16[8,6,16384]{2,1,0:T(8,128)(2,1)} async-done(((bf16[8,6,16384]{2,1,0:T(8,128)(2,1)}), bf16[8,6,16384]{2,1,0:T(8,128)(2,1)}, u32[]{:S(2)}, u32[]{:S(2)}) %all-to-all-start.3) | async-done | bytes 1572896 | tf_op jit(solution)/shard_map/all_to_all | solution.py:62
  170.1 14.9 %all-to-all-done.1 = bf16[8,6,16384]{2,1,0:T(8,128)(2,1)S(1)} async-done(((bf16[8,6,16384]{2,1,0:T(8,128)(2,1)}), bf16[8,6,16384]{2,1,0:T(8,128)(2,1)S(1)}, u32[]{:S(2)}, u32[]{:S(2)}) %all-to-all-start.1) | async-done | bytes 1572896 | tf_op jit(solution)/shard_map/all_to_all | solution.py:62
  189.4 35.9 %all-reduce = (f32[32]{0:T(128)S(1)}, f32[32]{0:T(128)S(1)}, f32[32]{0:T(128)S(1)}, f32[32]{0:T(128)S(1)}) all-reduce(f32[32]{0:T(128)S(1)} %convert_reduce_fusion, f32[32]{0:T(128)S(1)} %convert_reduce_fusion.1, f32[32]{0:T(128)S(1)} %convert_reduce_fusion.2, f32[32]{0:T(128)S(1)} %convert_reduce_fusion.3), channel_id=1, replica_groups=mesh['dom'=16,'cls'=8] {'dom'}, use_global_device_ids=true, to_apply=%region_22.24 | all-reduce | flops 128 | bytes 1024 | tf_op jit(solution)/shard_map/psum | solution.py:69
  225.3 166.9 %all-reduce.4.cloned.1.call-done = (f32[32,16384]{1,0:T(8,128)}, f32[32,16384]{1,0:T(8,128)}, f32[32,16384]{1,0:T(8,128)}, f32[32,16384]{1,0:T(8,128)}) async-done(((f32[32,16384]{1,0:T(8,128)}, f32[32,16384]{1,0:T(8,128)}, f32[32,16384]{1,0:T(8,128)}, f32[32,16384]{1,0:T(8,128)}), (f32[32,16384]{1,0:T(8,128)}, f32[32,16384]{1,0:T(8,128)}, f32[32,16384]{1,0:T(8,128)}, ...) | async-done | bytes 8388624 | tf_op jit(solution)/shard_map/psum | solution.py:69
  392.3 4.9 convert_select_fusion.2
  399.2 4.9 convert_select_fusion
  448.3 22.5 %copy.48 = bf16[16,32,128,128]{3,2,1,0:T(8,128)(2,1)} copy(bf16[16,32,128,128]{3,2,0,1:T(8,128)(2,1)} %get-tuple-element.17) | data formatting | bytes 33554432 | tf_op jit(solution)/shard_map/stack | solution.py:79
  470.9 14.2 %copy.55 = bf16[16,32,128,128]{3,2,1,0:T(8,128)(2,1)} copy(bf16[16,32,128,128]{3,2,0,1:T(8,128)(2,1)} %get-tuple-element.18) | data formatting | bytes 33554432 | tf_op jit(solution)/shard_map/stack | solution.py:79
  487.1 4.7 reduce_sum.122
  491.8 87.7 %all-gather.11.cloned.1.call-done = bf16[256,16384]{1,0:T(8,128)(2,1)} async-done(((bf16[32,16384]{1,0:T(8,128)(2,1)}), bf16[256,16384]{1,0:T(8,128)(2,1)}) %all-gather.11.cloned.1.call-update) | async-done | bytes 8388624 | tf_op jit(solution)/shard_map/all_gather | solution.py:16
  579.5 4.7 reduce_sum.125
  584.2 87.5 %all-gather.13.cloned.1.call-done = bf16[256,16384]{1,0:T(8,128)(2,1)} async-done(((bf16[32,16384]{1,0:T(8,128)(2,1)}), bf16[256,16384]{1,0:T(8,128)(2,1)}) %all-gather.13.cloned.1.call-update) | async-done | bytes 8388624 | tf_op jit(solution)/shard_map/all_gather | solution.py:16
  671.7 5.9 reduce_sum.128
  677.7 17.6 %fusion.14 = f32[512,32]{1,0:T(8,128)} fusion(bf16[32,16384]{1,0:T(8,128)(2,1)S(1)} %reduce_sum.122, bf16[64,8,128,128]{3,2,1,0:T(8,128)(2,1)} %bitcast.408), kind=kOutput, calls=%fused_computation.26 | convolution fusion | flops 536870912 | bytes 17891328 | tf_op jit(solution)/shard_map/dot_general | solution.py:80
  695.2 18.2 %fusion.6 = f32[512,32]{1,0:T(8,128)} fusion(bf16[32,16384]{1,0:T(8,128)(2,1)S(1)} %reduce_sum.122, bf16[64,8,128,128]{3,2,1,0:T(8,128)(2,1)} %bitcast.414), kind=kOutput, calls=%fused_computation.18 | convolution fusion | flops 536870912 | bytes 17891328 | tf_op jit(solution)/shard_map/dot_general | solution.py:80
  713.5 17.8 %fusion.12 = f32[512,32]{1,0:T(8,128)} fusion(bf16[32,16384]{1,0:T(8,128)(2,1)S(1)} %reduce_sum.125, bf16[64,8,128,128]{3,2,1,0:T(8,128)(2,1)S(1)} %bitcast.412), kind=kOutput, calls=%fused_computation.24 | convolution fusion | flops 536870912 | bytes 17891328 | tf_op jit(solution)/shard_map/dot_general | solution.py:80
  731.3 21.2 %fusion.4 = f32[512,32]{1,0:T(8,128)S(1)} fusion(bf16[32,16384]{1,0:T(8,128)(2,1)S(1)} %reduce_sum.125, bf16[64,8,128,128]{3,2,1,0:T(8,128)(2,1)} %bitcast.415), kind=kOutput, calls=%fused_computation.16 | convolution fusion | flops 536870912 | bytes 17891328 | tf_op jit(solution)/shard_map/dot_general | solution.py:80
  752.6 17.1 %fusion.10 = f32[512,32]{1,0:T(8,128)S(1)} fusion(bf16[32,16384]{1,0:T(8,128)(2,1)S(1)} %copy-done, bf16[64,8,128,128]{3,2,1,0:T(8,128)(2,1)S(1)} %bitcast.413), kind=kOutput, calls=%fused_computation.22 | convolution fusion | flops 536870912 | bytes 17891328 | tf_op jit(solution)/shard_map/dot_general | solution.py:80
  769.7 20.7 %fusion.2 = f32[512,32]{1,0:T(8,128)S(1)} fusion(bf16[32,16384]{1,0:T(8,128)(2,1)S(1)} %copy-done, bf16[64,8,128,128]{3,2,1,0:T(8,128)(2,1)} %bitcast.416), kind=kOutput, calls=%fused_computation.14 | convolution fusion | flops 536870912 | bytes 17891328 | tf_op jit(solution)/shard_map/dot_general | solution.py:80
  790.4 4.7 reduce_sum.131
  795.1 20.8 %fusion.8 = f32[512,32]{1,0:T(8,128)S(1)} fusion(bf16[32,16384]{1,0:T(8,128)(2,1)S(1)} %reduce_sum.131, bf16[64,8,128,128]{3,2,1,0:T(8,128)(2,1)} %bitcast.409), kind=kOutput, calls=%fused_computation.20 | convolution fusion | flops 536870912 | bytes 17891328 | tf_op jit(solution)/shard_map/dot_general | solution.py:80
  816.0 20.9 %fusion = f32[512,32]{1,0:T(8,128)S(1)} fusion(bf16[32,16384]{1,0:T(8,128)(2,1)S(1)} %reduce_sum.131, bf16[64,8,128,128]{3,2,1,0:T(8,128)(2,1)} %bitcast.417), kind=kOutput, calls=%fused_computation.12 | convolution fusion | flops 536870912 | bytes 17891328 | tf_op jit(solution)/shard_map/dot_general | solution.py:80
  (147 shorter events, 110.4 us)
Async XLA Ops:
  12.0 21.3 %all-to-all-start.6 = ((bf16[8,6,32]{2,1,0:T(8,128)(2,1)}), bf16[8,6,32]{2,1,0:T(8,128)(2,1)S(1)}, u32[]{:S(2)}, u32[]{:S(2)}) async-start(bf16[8,6,32]{2,1,0:T(8,128)(2,1)} %all_to_all.60), calls=%async_computation.6 | async-start | bytes 32768 | tf_op jit(solution)/shard_map/all_to_all | solution.py:63
  33.3 10.2 %all-to-all-start.4 = ((bf16[8,6,32]{2,1,0:T(8,128)(2,1)}), bf16[8,6,32]{2,1,0:T(8,128)(2,1)S(1)}, u32[]{:S(2)}, u32[]{:S(2)}) async-start(bf16[8,6,32]{2,1,0:T(8,128)(2,1)} %all_to_all.56), calls=%async_computation.4 | async-start | bytes 32768 | tf_op jit(solution)/shard_map/all_to_all | solution.py:63
  43.5 8.3 all-to-all-start.2
  51.9 8.3 all-to-all-start
  60.2 31.4 %all-to-all-start.7 = ((bf16[8,6,16384]{2,1,0:T(8,128)(2,1)}), bf16[8,6,16384]{2,1,0:T(8,128)(2,1)}, u32[]{:S(2)}, u32[]{:S(2)}) async-start(bf16[8,6,16384]{2,1,0:T(8,128)(2,1)} %all_to_all.62), calls=%async_computation.7 | async-start | bytes 4194304 | tf_op jit(solution)/shard_map/all_to_all | solution.py:62
  91.6 31.4 %all-to-all-start.5 = ((bf16[8,6,16384]{2,1,0:T(8,128)(2,1)}), bf16[8,6,16384]{2,1,0:T(8,128)(2,1)}, u32[]{:S(2)}, u32[]{:S(2)}) async-start(bf16[8,6,16384]{2,1,0:T(8,128)(2,1)} %all_to_all.58), calls=%async_computation.5 | async-start | bytes 4194304 | tf_op jit(solution)/shard_map/all_to_all | solution.py:62
  123.0 31.4 %all-to-all-start.3 = ((bf16[8,6,16384]{2,1,0:T(8,128)(2,1)}), bf16[8,6,16384]{2,1,0:T(8,128)(2,1)}, u32[]{:S(2)}, u32[]{:S(2)}) async-start(bf16[8,6,16384]{2,1,0:T(8,128)(2,1)} %all_to_all.54), calls=%async_computation.3 | async-start | bytes 4194304 | tf_op jit(solution)/shard_map/all_to_all | solution.py:62
  154.4 30.6 %all-to-all-start.1 = ((bf16[8,6,16384]{2,1,0:T(8,128)(2,1)}), bf16[8,6,16384]{2,1,0:T(8,128)(2,1)S(1)}, u32[]{:S(2)}, u32[]{:S(2)}) async-start(bf16[8,6,16384]{2,1,0:T(8,128)(2,1)} %all_to_all.50), calls=%async_computation.1 | async-start | bytes 4194304 | tf_op jit(solution)/shard_map/all_to_all | solution.py:62
  158.1 29.3 %copy-start.4 = (s32[4]{0:T(128)S(1)}, s32[4]{0:T(128)}, u32[]{:S(2)}) copy-start(s32[4]{0:T(128)} %param.17) | copy-start | bytes 52
  158.1 67.3 %copy-start.5 = (f32[32]{0:T(128)S(1)}, f32[32]{0:T(128)}, u32[]{:S(2)}) copy-start(f32[32]{0:T(128)} %param.12) | copy-start | bytes 388
  158.1 234.2 %all-reduce.4.cloned.1.call-start = ((), (), s32[]{:S(2)}) async-start(), calls=%async_computation.12 | async-start | bytes 16777216 | tf_op jit(solution)/shard_map/psum | solution.py:69
  187.3 299.8 %all-gather.9.cloned.1.call-start = ((), (), s32[]{:S(2)}) async-start(), calls=%async_computation.8 | async-start | bytes 9437184 | tf_op jit(solution)/shard_map/all_gather | solution.py:16
  397.2 182.3 %all-gather.11.cloned.1.call-start = ((), (), s32[]{:S(2)}) async-start(), calls=%async_computation.9 | async-start | bytes 9437184 | tf_op jit(solution)/shard_map/all_gather | solution.py:16
  397.9 273.8 %all-gather.13.cloned.1.call-start = ((), (), s32[]{:S(2)}) async-start(), calls=%async_computation.10 | async-start | bytes 9437184 | tf_op jit(solution)/shard_map/all_gather | solution.py:16
  404.1 386.3 %all-gather.15.cloned.1.call-start = ((), (), s32[]{:S(2)}) async-start(), calls=%async_computation.11 | async-start | bytes 9437184 | tf_op jit(solution)/shard_map/all_gather | solution.py:16
  677.7 35.8 %slice-start = ((s8[16777216]{0:T(1024)(128)(4,1)}), s8[4194304]{0:T(1024)(128)(4,1)S(1)}, s32[]{:S(2)}) async-start(s8[16777216]{0:T(1024)(128)(4,1)} %bitcast.410), calls=%async_computation.13 | async-start | bytes 8388608
  677.7 35.8 %slice-start.1 = ((s8[16777216]{0:T(1024)(128)(4,1)}), s8[4194304]{0:T(1024)(128)(4,1)S(1)}, s32[]{:S(2)}) async-start(s8[16777216]{0:T(1024)(128)(4,1)} %bitcast.410), calls=%async_computation.14 | async-start | bytes 8388608
  695.2 18.2 %slice-start.2 = ((s8[16777216]{0:T(1024)(128)(4,1)}), s8[4194304]{0:T(1024)(128)(4,1)S(1)}, s32[]{:S(2)}) async-start(s8[16777216]{0:T(1024)(128)(4,1)} %bitcast.410), calls=%async_computation.15 | async-start | bytes 8388608
  695.2 18.2 %slice-start.3 = ((s8[16777216]{0:T(1024)(128)(4,1)}), s8[4194304]{0:T(1024)(128)(4,1)S(1)}, s32[]{:S(2)}) async-start(s8[16777216]{0:T(1024)(128)(4,1)} %bitcast.410), calls=%async_computation.16 | async-start | bytes 8388608
  731.3 21.3 %copy-start = (bf16[32,16384]{1,0:T(8,128)(2,1)S(1)}, bf16[32,16384]{1,0:T(8,128)(2,1)}, u32[]{:S(2)}) copy-start(bf16[32,16384]{1,0:T(8,128)(2,1)} %reduce_sum.128) | copy-start | bytes 3145732
  815.9 20.9 %copy-start.3 = (f32[512,32]{1,0:T(8,128)S(1)}, f32[512,32]{1,0:T(8,128)}, u32[]{:S(2)}) copy-start(f32[512,32]{1,0:T(8,128)} %fusion.14) | copy-start | bytes 196612
  815.9 21.0 %copy-start.1 = (f32[512,32]{1,0:T(8,128)S(1)}, f32[512,32]{1,0:T(8,128)}, u32[]{:S(2)}) copy-start(f32[512,32]{1,0:T(8,128)} %fusion.6) | copy-start | bytes 196612
  816.0 21.2 %copy-start.2 = (f32[512,32]{1,0:T(8,128)S(1)}, f32[512,32]{1,0:T(8,128)}, u32[]{:S(2)}) copy-start(f32[512,32]{1,0:T(8,128)} %fusion.12) | copy-start | bytes 196612
Sparse Core Ops, SparseCore 0:
  187.4 204.7 all-reduce.3
  397.3 89.7 all-gather.8
  488.8 90.6 all-gather.10
  581.0 90.6 all-gather.12
  673.2 90.6 all-gather.14
